TPU v7x, 512 devices: a whole 4x4x16 slice. The times are simulated.
512 devices in a mesh: ax: 32 (over z, x_hi), pen: 16 (over x_lo, y, core).
Axes of the slice: x: 4 (x_hi: 2, x_lo: 2; x = x_hi * 2 + x_lo), y: 4, z: 16, core: 2. Of those that a mesh axis runs over, the one named last changes fastest.
Arguments:
- fields: float32 [2, 5, 512, 192, 128], P(None, None, 'ax', 'pen'), may hold values from -0.8 to 0.8, as said below
- axial_mean: float32 [512, 192, 128], P('ax', 'pen'), may hold values from 0.2 to 1.5
- radial_mean: float32 [512, 192, 128], P('ax', 'pen'), may hold values from -0.3 to 0.3
- swirl_mean: float32 [512, 192, 128], P('ax', 'pen'), may hold values from -0.3 to 0.3
- density: float32 [512, 192, 128], P('ax', 'pen'), may hold values from 0.5 to 2
- pressure: float32 [512, 192, 128], P('ax', 'pen'), may hold values from 0.4 to 1.2
Outputs:
- residual: float32 [2, 5, 512, 192, 128], P(None, None, 'ax', 'pen')
Inputs may be any that keep to these rules, and one draw needn't show every extreme that they name: `fields`: each entry is a draw times (1 - c_j^2)^2 with c_j = cos(pi j / 191) at radial node j, so every field vanishes at both radial ends.
All inputs are finite; a program needn't handle non-finite values.
Results may differ from a plain program's by a relative error of at most 0.0001.
Values sent between devices are 32-bit elements; how exact they have to be, the bound alone decides.
No kernel may reach another device: no remote copies, remote signals or barrier semaphores. Data moves between devices by JAX's collectives and lax.ppermute only.
A program may use at most 64 MiB of HBM per device.

v0:
```python
import jax
import jax.numpy as jnp
import numpy as np
from jax import lax
from jax.sharding import PartitionSpec as P

angular_frequency = 1.7
viscosity = 0.01
conduction = 0.014
gamma_ratio = 1.4
spacing = 0.1
radius_inner = 0.5
radius_outer = 6.5
first_axial = (0.8, -0.2, 4.0 / 105.0, -1.0 / 280.0)
axial_second_derivative = (-205.0 / 72.0, 1.6, -0.2, 8.0 / 315.0, -1.0 / 560.0)
highest = lax.Precision.HIGHEST


def with_halo(array, sides, width):
    for axis, dim in sides:
        size, length = (lax.axis_size(axis), array.shape[dim])
        up = [(i, (i + 1) % size) for i in range(size - 1)]
        down = [(j, i) for i, j in up]
        last = lax.slice_in_dim(array, length - width, length, axis=dim)
        initial = lax.slice_in_dim(array, 0, width, axis=dim)
        before = lax.ppermute(last, axis, up)
        after = lax.ppermute(initial, axis, down)
        array = jnp.concatenate([before, array, after], axis=dim)
    return array


def cheb_tables(node_count):
    last_node = node_count - 1
    node_index = np.arange(node_count)
    cheb_nodes = np.cos(np.pi * node_index / last_node)
    end_weight = np.where((node_index == 0) | (node_index == last_node), 2.0, 1.0) * np.where(
        node_index % 2 == 0, 1.0, -1.0
    )
    row_index = node_index[:, None]
    col_index = node_index[None, :]
    node_gap = (
        -2.0
        * np.sin(np.pi * (row_index + col_index) / (2 * last_node))
        * np.sin(np.pi * (row_index - col_index) / (2 * last_node))
    )
    off_diag = row_index != col_index
    safe_gap = np.where(off_diag, node_gap, 1.0)
    matrix = np.where(off_diag, end_weight[:, None] / end_weight[None, :] / safe_gap, 0.0)
    row_total = matrix.sum(axis=1)
    matrix = np.where(off_diag, matrix, -row_total[:, None])
    order_first_terms = matrix * (-2.0 / (radius_outer - radius_inner))
    second_order = order_first_terms @ order_first_terms
    radius_nodes = radius_inner + (radius_outer - radius_inner) * (1.0 - cheb_nodes) / 2.0
    return (order_first_terms, second_order, radius_nodes)


def fourier_tables(point_count):
    offsets = np.arange(point_count)[:, None] - np.arange(point_count)[None, :]
    half_angle = np.pi * offsets / point_count
    sign_table = np.where(offsets % 2 == 0, 1.0, -1.0)
    nonzero = offsets != 0
    safe_sine = np.where(nonzero, np.sin(half_angle), 1.0)
    order_first_terms = np.where(nonzero, 0.5 * sign_table * np.cos(half_angle) / safe_sine, 0.0)
    second_order = np.where(
        nonzero, -0.5 * sign_table / safe_sine**2, -(point_count**2) / 12.0 - 1.0 / 6.0
    )
    return (order_first_terms, second_order)


def build_work(fields, density, pressure):
    thermal_field = fields[:, 4] / density - pressure * fields[:, 3] / (density * density)
    return jnp.concatenate([fields[:, :3], thermal_field[:, None], fields[:, 3:]], axis=1)


def axial_derivatives(padded, planes):

    def shifted(source, offset):
        return lax.slice_in_dim(source, 4 + offset, 4 + offset + planes, axis=2)

    lower = padded[:, :4]
    slope_x = first_axial[0] * (shifted(padded, 1) - shifted(padded, -1))
    curve_x = axial_second_derivative[0] * shifted(lower, 0)
    for offset in range(1, 5):
        if offset > 1:
            slope_x = slope_x + first_axial[offset - 1] * (
                shifted(padded, offset) - shifted(padded, -offset)
            )
        curve_x = curve_x + axial_second_derivative[offset] * (
            shifted(lower, offset) + shifted(lower, -offset)
        )
    return (slope_x / spacing, curve_x / (spacing * spacing))


def theta_derivatives(work_fields, theta_first, azimuthal_second_derivative):
    slope_t = jnp.dot(work_fields, theta_first, precision=highest)
    curve_t = jnp.dot(work_fields[:, :4], azimuthal_second_derivative, precision=highest)
    return (slope_t, curve_t)


def radial_derivatives(pencil_block, radial_first, radial_second):
    slope_r = jnp.einsum("sj,abxjt->abxst", radial_first, pencil_block, precision=highest)
    curve_r = jnp.einsum("sj,abxjt->abxst", radial_second, pencil_block[:, :4], precision=highest)
    return (slope_r, curve_r)


def rotate_phase(value):
    return jnp.stack([-angular_frequency * value[1], angular_frequency * value[0]])


def radial_terms(slope_r, curve_r, radial_mean, density, pressure, inv_radius):
    laplace = curve_r + slope_r[:, :4] * inv_radius
    convect = radial_mean * slope_r
    term_u = convect[:, 0] - viscosity * laplace[:, 0]
    term_v = convect[:, 1] + slope_r[:, 5] / density - viscosity * laplace[:, 1]
    term_w = convect[:, 2] - viscosity * laplace[:, 2]
    term_rho = convect[:, 4] + density * slope_r[:, 1]
    term_p = convect[:, 5] + gamma_ratio * pressure * slope_r[:, 1] - conduction * laplace[:, 3]
    return jnp.stack([term_u, term_v, term_w, term_rho, term_p], axis=1)


def other_terms(
    work_fields,
    slope_x,
    curve_x,
    slope_t,
    curve_t,
    axial_mean,
    radial_mean,
    swirl_mean,
    density,
    pressure,
    inv_radius,
):
    inv_square = inv_radius * inv_radius
    convect = axial_mean * slope_x + swirl_mean * inv_radius * slope_t
    laplace = curve_x + inv_square * curve_t
    vel_u = work_fields[:, 0]
    vel_v = work_fields[:, 1]
    vel_w = work_fields[:, 2]
    div_part = slope_x[:, 0] + inv_radius * (vel_v + slope_t[:, 2])
    term_u = (
        rotate_phase(vel_u) + convect[:, 0] + slope_x[:, 5] / density - viscosity * laplace[:, 0]
    )
    term_v = (
        rotate_phase(vel_v)
        + convect[:, 1]
        - 2.0 * swirl_mean * inv_radius * vel_w
        - viscosity * (laplace[:, 1] - inv_square * (vel_v + 2.0 * slope_t[:, 2]))
    )
    term_w = (
        rotate_phase(vel_w)
        + convect[:, 2]
        + inv_radius * slope_t[:, 5] / density
        + inv_radius * (radial_mean * vel_w + swirl_mean * vel_v)
        - viscosity * (laplace[:, 2] - inv_square * (vel_w - 2.0 * slope_t[:, 1]))
    )
    term_rho = rotate_phase(work_fields[:, 4]) + convect[:, 4] + density * div_part
    term_p = (
        rotate_phase(work_fields[:, 5])
        + convect[:, 5]
        + gamma_ratio * pressure * div_part
        - conduction * laplace[:, 3]
    )
    return jnp.stack([term_u, term_v, term_w, term_rho, term_p], axis=1)


def per_device(fields, axial_mean, radial_mean, swirl_mean, density, pressure):
    planes = fields.shape[2]
    shard_rows = fields.shape[3]
    grid_points = fields.shape[4]
    total_rows = shard_rows * lax.axis_size("pen")
    first_np, second_np, radius_np = cheb_tables(total_rows)
    radial_first = jnp.asarray(first_np, jnp.float32)
    radial_second = jnp.asarray(second_np, jnp.float32)
    inv_all = jnp.asarray(1.0 / radius_np, jnp.float32)[:, None]
    inv_local = lax.dynamic_slice_in_dim(inv_all, lax.axis_index("pen") * shard_rows, shard_rows, 0)
    theta_np, theta_second_np = fourier_tables(grid_points)
    theta_first = jnp.asarray(theta_np.T, jnp.float32)
    azimuthal_second_derivative = jnp.asarray(theta_second_np.T, jnp.float32)
    work_fields = build_work(fields, density, pressure)
    padded = with_halo(work_fields, (("ax", 2),), 4)
    slope_x, curve_x = axial_derivatives(padded, planes)
    slope_t, curve_t = theta_derivatives(work_fields, theta_first, azimuthal_second_derivative)
    slope_r, curve_r = radial_derivatives(
        lax.all_to_all(work_fields, "pen", split_axis=2, concat_axis=3, tiled=True),
        radial_first,
        radial_second,
    )
    slope_r, curve_r = (
        lax.all_to_all(slope_r, "pen", split_axis=3, concat_axis=2, tiled=True),
        lax.all_to_all(curve_r, "pen", split_axis=3, concat_axis=2, tiled=True),
    )
    radial_component = radial_terms(slope_r, curve_r, radial_mean, density, pressure, inv_local)
    return radial_component + other_terms(
        work_fields,
        slope_x,
        curve_x,
        slope_t,
        curve_t,
        axial_mean,
        radial_mean,
        swirl_mean,
        density,
        pressure,
        inv_local,
    )


def solution(mesh):
    placed = (
        P(None, None, "ax", "pen", None),
        P("ax", "pen", None),
        P("ax", "pen", None),
        P("ax", "pen", None),
        P("ax", "pen", None),
        P("ax", "pen", None),
    )
    return jax.shard_map(
        per_device,
        mesh=mesh,
        in_specs=placed,
        out_specs=P(None, None, "ax", "pen", None),
        check_vma=False,
    )
```

profile of v0, /device:TPU:4, one launch (start us, length us, event | category | flops | bytes accessed | tf_op | source)
XLA Modules:
  0.0 97.6 jit_solution(14125094061628838863)
XLA Ops:
  0.0 1.2 %slice.244 = f32[2,3,16,12,128]{4,2,3,1,0:T(8,128)S(1)} slice(f32[2,5,16,12,128]{4,2,3,1,0:T(8,128)} %param.11), slice={[0:2], [0:3], [0:16], [0:12], [0:128]} | slice | bytes 1179648 | tf_op jit(solution)/shard_map/slice | solution.py:72
  1.6 2.0 %copy.44 = f32[2,6,16,12,128]{4,0,3,1,2:T(2,128)} copy(f32[2,6,16,12,128]{4,2,3,1,0:T(8,128)S(1)} %pad_maximum_fusion.1) | data formatting | bytes 2359296 | tf_op jit(solution)/shard_map/concatenate | solution.py:72
  3.6 5.3 %all-to-all-start = ((f32[2,6,16,12,128]{4,0,3,1,2:T(2,128)}), f32[2,6,16,12,128]{4,0,3,1,2:T(2,128)}, u32[]{:S(2)}, u32[]{:S(2)}) async-start(f32[2,6,16,12,128]{4,0,3,1,2:T(2,128)} %copy.44), calls=%async_computation | async-start | bytes 2359296 | tf_op jit(solution)/shard_map/all_to_all | solution.py:185
  8.9 0.9 fusion.53
  9.8 6.9 %collective-permute-start = (f32[2,6,4,12,128]{4,2,3,1,0:T(4,128)}, f32[2,6,4,12,128]{4,2,3,1,0:T(4,128)S(1)}, u32[]{:S(2)}, u32[]{:S(2)}) collective-permute-start(f32[2,6,4,12,128]{4,2,3,1,0:T(4,128)} %get-tuple-element.11), channel_id=1, source_target_pairs={{16,0},{32,16},{48,32},{64,48},{80,64},{96,80},{112,96},{128,112},... | collective-permute-start | bytes 884744 | tf_op jit(solution)/shard_map/ppermute | solution.py:27
  16.7 1.9 %collective-permute-start.1 = (f32[2,6,4,12,128]{4,2,3,1,0:T(4,128)}, f32[2,6,4,12,128]{4,2,3,1,0:T(4,128)S(1)}, u32[]{:S(2)}, u32[]{:S(2)}) collective-permute-start(f32[2,6,4,12,128]{4,2,3,1,0:T(4,128)} %get-tuple-element.12), channel_id=1, source_target_pairs={{0,16},{16,32},{32,48},{48,64},{64,80},{80,96},{96,112},{112,128},... | collective-permute-start | bytes 884744 | tf_op jit(solution)/shard_map/ppermute | solution.py:26
  18.7 1.7 %broadcast_multiply_fusion.2 = (f32[16,12,128]{2,0,1:T(8,128)}, f32[16,12,128]{2,0,1:T(8,128)}, f32[16,12,128]{2,0,1:T(8,128)}) fusion(f32[16,12,128]{2,0,1:T(8,128)S(1)} %copy-done.8, f32[12]{0:T(128)S(1)} %get-tuple-element.30, f32[12]{0:T(128)S(1)} %get-tuple-element.32, f32[16,12,128]{2,0,1:T(8,128)} %param.12), kind=kLoop, calls=%fused_computation.100 | loop fusion | flops 73728 | bytes 491616 | tf_op jit(solution)/shard_map/mul | solution.py:147
  20.4 0.9 broadcast_multiply_fusion.5
  21.3 1.0 slice_multiply_fusion.10
  22.3 6.7 %collective-permute-done = f32[2,6,4,12,128]{4,2,3,1,0:T(4,128)S(1)} collective-permute-done((f32[2,6,4,12,128]{4,2,3,1,0:T(4,128)}, f32[2,6,4,12,128]{4,2,3,1,0:T(4,128)S(1)}, u32[]{:S(2)}, u32[]{:S(2)}) %collective-permute-start) | collective-permute-done | bytes 294944 | tf_op jit(solution)/shard_map/ppermute | solution.py:27
  28.9 11.4 %collective-permute-done.1 = f32[2,6,4,12,128]{4,2,3,1,0:T(4,128)S(1)} collective-permute-done((f32[2,6,4,12,128]{4,2,3,1,0:T(4,128)}, f32[2,6,4,12,128]{4,2,3,1,0:T(4,128)S(1)}, u32[]{:S(2)}, u32[]{:S(2)}) %collective-permute-start.1) | collective-permute-done | bytes 294944 | tf_op jit(solution)/shard_map/ppermute | solution.py:26
  40.4 2.1 %pad_maximum_fusion = (f32[2,6,20,12,128]{4,2,3,1,0:T(8,128)}, f32[2,6,20,12,128]{4,2,3,1,0:T(8,128)}) fusion(f32[2,6,4,12,128]{4,2,3,1,0:T(4,128)S(1)} %collective-permute-done, f32[2,2,16,12,128]{4,2,3,1,0:T(8,128)S(1)} %slice.247, f32[2,1,16,12,128]{4,2,3,1,0:T(8,128)S(1)} %divide_subtract_fusion, f32[2,3,16,12,128]{4,2,3,1,0:T(8,128)S(1)} %slice.244, ...), kind=kLoop, calls=%fused_computation | loop fusion | flops 2211840 | bytes 4718592 | tf_op jit(solution)/shard_map/concatenate | solution.py:28
  42.5 1.4 %copy.45 = f32[2,6,16,12,128]{4,0,3,2,1:T(2,128)S(1)} copy(f32[2,6,16,12,128]{4,0,3,1,2:T(2,128)} %all-to-all-done) | data formatting | bytes 2359296 | tf_op jit(solution)/shard_map/all_to_all | solution.py:185
  43.9 1.2 %convolution_bitcast_fusion = f32[2,6,1,192,128]{4,3,1,0,2:T(8,128)S(1)} fusion(f32[192,192,1,1]{1,0,3,2:T(8,128)S(1)} %copy-done.24, f32[2,6,192,128]{3,0,2,1:T(2,128)S(1)} %bitcast.35), kind=kOutput, calls=%fused_computation.2 | convolution fusion | flops 679477248 | bytes 2506752 | tf_op jit(solution)/shard_map/sj,abxjt->abxst/dot_general | solution.py:101
  45.1 1.9 %copy.47 = f32[2,6,1,192,128]{4,0,2,1,3:T(2,128)} copy(f32[2,6,1,192,128]{4,3,1,0,2:T(8,128)S(1)} %convolution_bitcast_fusion) | data formatting | bytes 2359296 | tf_op jit(solution)/shard_map/sj,abxjt->abxst/transpose | solution.py:101
  47.1 6.2 %all-to-all-start.1 = ((f32[2,6,1,192,128]{4,0,2,1,3:T(2,128)}), f32[2,6,1,192,128]{4,0,2,1,3:T(2,128)}, u32[]{:S(2)}, u32[]{:S(2)}) async-start(f32[2,6,1,192,128]{4,0,2,1,3:T(2,128)} %copy.47), calls=%async_computation.1 | async-start | bytes 2359296 | tf_op jit(solution)/shard_map/all_to_all | solution.py:190
  53.3 8.7 %multiply_add_fusion = (f32[2,6,16,12,128]{4,2,3,1,0:T(8,128)S(1)}, f32[2,6,16,12,128]{4,2,3,1,0:T(8,128)S(1)}, f32[2,6,16,12,128]{4,2,3,1,0:T(8,128)}) fusion(f32[16,12,128]{2,0,1:T(8,128)} %get-tuple-element.29, f32[16,12,128]{2,0,1:T(8,128)} %get-tuple-element.34, f32[2,6,20,12,128]{4,2,3,1,0:T(8,128)} %get-tuple-element.10, ...), kind=kOutput, calls=%fused_computation.19 | convolution fusion | flops 457703424 | bytes 14417920 | tf_op jit(solution)/shard_map/dot_general | solution.py:95
  62.1 0.8 copy-done.26
  62.9 5.3 %fusion = f32[2,4,16,12,128]{4,2,3,1,0:T(8,128)S(1)} fusion(f32[128,128,1,1,1]{1,0,4,3,2:T(8,128)S(1)} %copy-done.26, f32[2,6,20,12,128]{4,2,3,1,0:T(8,128)} %get-tuple-element.10, f32[2,6,20,12,128]{4,2,3,1,0:T(8,128)} %get-tuple-element.9, f32[2,1,16,12,128]{4,2,3,1,0:T(8,128)S(1)} %divide_subtract_fusion, f32[2,3,16,12,128]{4,2,3,1,0:T(8,128)S(1)} %slice.244, ...), kind=kOutput, calls=%fused_computation.5 | convolution fusion | flops 305528832 | bytes 8716800 | tf_op jit(solution)/shard_map/dot_general | solution.py:96
  69.4 0.9 convolution_bitcast_fusion.1
  70.3 1.4 %copy.52 = f32[2,4,1,192,128]{4,1,0,2,3:T(4,128)} copy(f32[2,4,1,192,128]{4,3,1,0,2:T(8,128)S(1)} %convolution_bitcast_fusion.1) | data formatting | bytes 1572864 | tf_op jit(solution)/shard_map/sj,abxjt->abxst/transpose | solution.py:102
  71.7 5.9 %all-to-all-start.2 = ((f32[2,4,1,192,128]{4,1,0,2,3:T(4,128)}), f32[2,4,1,192,128]{4,1,0,2,3:T(4,128)}, u32[]{:S(2)}, u32[]{:S(2)}) async-start(f32[2,4,1,192,128]{4,1,0,2,3:T(4,128)} %copy.52), calls=%async_computation.2 | async-start | bytes 1572864 | tf_op jit(solution)/shard_map/all_to_all | solution.py:191
  77.6 1.2 %fusion.35 = f32[2,5,16,12,128]{4,2,3,1,0:T(8,128)S(1)} fusion(f32[2,5,16,12,128]{4,2,3,1,0:T(8,128)S(1)} %fusion.38, f32[2,4,16,12,128]{4,2,3,1,0:T(8,128)S(1)} %copy-done.7, f32[2,6,16,12,128]{4,2,3,1,0:T(8,128)} %copy-done.5, f32[1,1,16,12,128]{4,2,3,1,0:T(8,128)S(1)} %copy-done.22, f32[1,1,16,12,128]{4,2,3,1,0:T(8,128)} %get-tuple-element.20, ...), kind=kLoop, calls=%fused_computation.63 | loop fusion | flops 491520 | bytes 1475072
  78.9 1.3 %fusion.29 = f32[2,5,16,12,128]{4,2,3,1,0:T(8,128)S(1)} fusion(f32[2,5,16,12,128]{4,2,3,1,0:T(8,128)S(1)} %fusion.35, f32[2,6,16,12,128]{4,2,3,1,0:T(8,128)} %get-tuple-element.33, f32[2,4,16,12,128]{4,2,3,1,0:T(8,128)S(1)} %copy-done.7, f32[2,6,16,12,128]{4,2,3,1,0:T(8,128)} %copy-done.5, f32[1,1,16,12,128]{4,2,3,1,0:T(8,128)S(1)} %copy-done.16, ...), kind=kLoop, calls=%fused_computation.54 | loop fusion | flops 786432 | bytes 1868800
  80.1 0.9 copy-done.3
  81.1 1.7 %broadcast_multiply_fusion.1 = (f32[2,6,16,12,128]{4,2,3,1,0:T(8,128)S(1)}, f32[2,6,16,12,128]{4,2,3,1,0:T(8,128)S(1)}) fusion(f32[16,12,128]{2,0,1:T(8,128)S(1)} %copy-done.11, f32[2,6,16,12,128]{4,0,1,3,2:T(2,128)} %bitcast.6), kind=kLoop, calls=%fused_computation.38 | loop fusion | flops 294912 | bytes 3637248 | tf_op jit(solution)/shard_map/mul | solution.py:112
  82.7 8.6 %all-to-all-done.2 = f32[2,4,1,192,128]{4,1,0,2,3:T(4,128)} async-done(((f32[2,4,1,192,128]{4,1,0,2,3:T(4,128)}), f32[2,4,1,192,128]{4,1,0,2,3:T(4,128)}, u32[]{:S(2)}, u32[]{:S(2)}) %all-to-all-start.2) | async-done | bytes 786464 | tf_op jit(solution)/shard_map/all_to_all | solution.py:191
  91.4 1.7 %fusion.18 = f32[2,4,16,12,128]{4,2,3,1,0:T(8,128)S(1)} fusion(f32[2,6,16,12,128]{4,2,3,1,0:T(8,128)S(1)} %get-tuple-element.14, f32[2,4,16,12,128]{4,1,0,3,2:T(4,128)} %bitcast.13, f32[12]{0:T(128)S(1)} %get-tuple-element.32), kind=kLoop, calls=%fused_computation.34 | loop fusion | flops 393216 | bytes 2359344 | tf_op jit(solution)/shard_map/add | solution.py:111
  93.2 1.2 %fusion.23 = (f32[2,5,16,12,128]{4,2,3,1,0:T(8,128)S(1)}, f32[2,1,16,12,128]{4,2,3,1,0:T(8,128)S(1)}, f32[2,5,16,12,128]{4,2,3,1,0:T(8,128)S(1)}) fusion(f32[2,5,16,12,128]{4,2,3,1,0:T(8,128)S(1)} %copy-done.4, f32[2,6,16,12,128]{4,2,3,1,0:T(8,128)} %copy-done.5, f32[1,1,16,12,128]{4,2,3,1,0:T(8,128)S(1)} %copy-done.15, ...), kind=kLoop, calls=%fused_computation.47 | loop fusion | flops 540672 | bytes 2261504
  94.5 0.8 copy-done.12
  95.3 1.1 %fusion.20 = (f32[2,5,16,12,128]{4,2,3,1,0:T(8,128)S(1)}, f32[2,5,16,12,128]{4,2,3,1,0:T(8,128)S(1)}) fusion(f32[2,5,16,12,128]{4,2,3,1,0:T(8,128)S(1)} %get-tuple-element.5, f32[2,4,16,12,128]{4,2,3,1,0:T(8,128)} %copy-done.6, f32[2,6,16,12,128]{4,2,3,1,0:T(8,128)} %copy-done.5, f32[1,1,16,12,128]{4,2,3,1,0:T(8,128)S(1)} %copy-done.13, ...), kind=kLoop, calls=%fused_computation.41 | loop fusion | flops 491520 | bytes 1867776 | tf_op jit(solution)/shard_map/stack | solution.py:164
  96.5 1.1 %add.150 = f32[2,5,16,12,128]{4,2,3,1,0:T(8,128)} add(f32[2,5,16,12,128]{4,2,3,1,0:T(8,128)S(1)} %get-tuple-element.26, f32[2,5,16,12,128]{4,2,3,1,0:T(8,128)S(1)} %get-tuple-element.25) | non-fusion elementwise | flops 245760 | bytes 2949120 | tf_op jit(solution)/shard_map/add | solution.py:194
  (64 shorter events, 1.9 us)
Async XLA Ops:
  0.0 1.4 %copy-start = (f32[2,5,16,12,128]{4,2,3,1,0:T(8,128)S(1)}, f32[2,5,16,12,128]{4,2,3,1,0:T(8,128)}, u32[]{:S(2)}) copy-start(f32[2,5,16,12,128]{4,2,3,1,0:T(8,128)} %param.11) | copy-start | bytes 2949124
  0.0 1.4 %copy-start.1 = (f32[16,12,128]{2,0,1:T(8,128)S(1)}, f32[16,12,128]{2,0,1:T(8,128)}, u32[]{:S(2)}) copy-start(f32[16,12,128]{2,0,1:T(8,128)} %param.15) | copy-start | bytes 294916
  0.0 1.4 %copy-start.18 = (f32[16,12,128]{2,0,1:T(8,128)S(1)}, f32[16,12,128]{2,0,1:T(8,128)}, u32[]{:S(2)}) copy-start(f32[16,12,128]{2,0,1:T(8,128)} %param.16) | copy-start | bytes 294916
  3.6 38.9 %all-to-all-start = ((f32[2,6,16,12,128]{4,0,3,1,2:T(2,128)}), f32[2,6,16,12,128]{4,0,3,1,2:T(2,128)}, u32[]{:S(2)}, u32[]{:S(2)}) async-start(f32[2,6,16,12,128]{4,0,3,1,2:T(2,128)} %copy.44), calls=%async_computation | async-start | bytes 2359296 | tf_op jit(solution)/shard_map/all_to_all | solution.py:185
  8.8 9.8 %copy-start.25 = (f32[192]{0:T(256)S(1)}, f32[192]{0:T(256)}, u32[]{:S(2)}) copy-start(f32[192]{0:T(256)} %constant.58.clone) | copy-start | bytes 2308
  8.8 9.8 %copy-start.8 = (f32[16,12,128]{2,0,1:T(8,128)S(1)}, f32[16,12,128]{2,0,1:T(8,128)}, u32[]{:S(2)}) copy-start(f32[16,12,128]{2,0,1:T(8,128)} %param.14) | copy-start | bytes 294916
  9.8 19.2 %collective-permute-start = (f32[2,6,4,12,128]{4,2,3,1,0:T(4,128)}, f32[2,6,4,12,128]{4,2,3,1,0:T(4,128)S(1)}, u32[]{:S(2)}, u32[]{:S(2)}) collective-permute-start(f32[2,6,4,12,128]{4,2,3,1,0:T(4,128)} %get-tuple-element.11), channel_id=1, source_target_pairs={{16,0},{32,16},{48,32},{64,48},{80,64},{96,80},{112,96},{128,112},... | collective-permute-start | bytes 884744 | tf_op jit(solution)/shard_map/ppermute | solution.py:27
  16.7 23.7 %collective-permute-start.1 = (f32[2,6,4,12,128]{4,2,3,1,0:T(4,128)}, f32[2,6,4,12,128]{4,2,3,1,0:T(4,128)S(1)}, u32[]{:S(2)}, u32[]{:S(2)}) collective-permute-start(f32[2,6,4,12,128]{4,2,3,1,0:T(4,128)} %get-tuple-element.12), channel_id=1, source_target_pairs={{0,16},{16,32},{32,48},{48,64},{64,80},{80,96},{96,112},{112,128},... | collective-permute-start | bytes 884744 | tf_op jit(solution)/shard_map/ppermute | solution.py:26
  42.5 1.4 %copy-start.24 = (f32[192,192,1,1]{1,0,3,2:T(8,128)S(1)}, f32[192,192,1,1]{1,0,3,2:T(8,128)}, u32[]{:S(2)}) copy-start(f32[192,192,1,1]{1,0,3,2:T(8,128)} %constant.67) | copy-start | bytes 442372
  47.1 24.6 %all-to-all-start.1 = ((f32[2,6,1,192,128]{4,0,2,1,3:T(2,128)}), f32[2,6,1,192,128]{4,0,2,1,3:T(2,128)}, u32[]{:S(2)}, u32[]{:S(2)}) async-start(f32[2,6,1,192,128]{4,0,2,1,3:T(2,128)} %copy.47), calls=%async_computation.1 | async-start | bytes 2359296 | tf_op jit(solution)/shard_map/all_to_all | solution.py:190
  62.0 6.2 %copy-start.5 = (f32[2,6,16,12,128]{4,2,3,1,0:T(8,128)}, f32[2,6,16,12,128]{4,2,3,1,0:T(8,128)S(1)}, u32[]{:S(2)}) copy-start(f32[2,6,16,12,128]{4,2,3,1,0:T(8,128)S(1)} %get-tuple-element.7) | copy-start | bytes 3538948
  62.0 0.9 copy-start.26
  62.1 6.1 %copy-start.2 = (f32[2,6,16,12,128]{4,2,3,1,0:T(8,128)}, f32[2,6,16,12,128]{4,2,3,1,0:T(8,128)S(1)}, u32[]{:S(2)}) copy-start(f32[2,6,16,12,128]{4,2,3,1,0:T(8,128)S(1)} %broadcast_multiply_fusion) | copy-start | bytes 3538948
  62.9 5.4 %copy-start.19 = (f32[1,1,16,12,128]{4,2,3,1,0:T(8,128)S(1)}, f32[1,1,16,12,128]{4,2,3,1,0:T(8,128)}, u32[]{:S(2)}) copy-start(f32[1,1,16,12,128]{4,2,3,1,0:T(8,128)} %get-tuple-element.21) | copy-start | bytes 294916
  62.9 5.4 %copy-start.20 = (f32[1,1,16,12,128]{4,2,3,1,0:T(8,128)S(1)}, f32[1,1,16,12,128]{4,2,3,1,0:T(8,128)}, u32[]{:S(2)}) copy-start(f32[1,1,16,12,128]{4,2,3,1,0:T(8,128)} %get-tuple-element.22) | copy-start | bytes 294916
  68.2 0.9 copy-start.6
  68.3 1.2 %copy-start.23 = (f32[192,192,1,1]{1,0,3,2:T(8,128)S(1)}, f32[192,192,1,1]{1,0,3,2:T(8,128)}, u32[]{:S(2)}) copy-start(f32[192,192,1,1]{1,0,3,2:T(8,128)} %constant.68) | copy-start | bytes 442372
  71.7 5.9 %copy-start.7 = (f32[2,4,16,12,128]{4,2,3,1,0:T(8,128)S(1)}, f32[2,4,16,12,128]{4,2,3,1,0:T(8,128)}, u32[]{:S(2)}) copy-start(f32[2,4,16,12,128]{4,2,3,1,0:T(8,128)} %copy-done.6) | copy-start | bytes 2359300
  71.7 5.9 %copy-start.21 = (f32[16,12,128]{2,0,1:T(8,128)S(1)}, f32[16,12,128]{2,0,1:T(8,128)}, u32[]{:S(2)}) copy-start(f32[16,12,128]{2,0,1:T(8,128)} %get-tuple-element.28) | copy-start | bytes 294916
  71.7 5.9 %copy-start.22 = (f32[1,1,16,12,128]{4,2,3,1,0:T(8,128)S(1)}, f32[1,1,16,12,128]{4,2,3,1,0:T(8,128)}, u32[]{:S(2)}) copy-start(f32[1,1,16,12,128]{4,2,3,1,0:T(8,128)} %get-tuple-element.19) | copy-start | bytes 294916
  71.7 7.1 %copy-start.9 = (f32[16,12,128]{2,0,1:T(8,128)S(1)}, f32[16,12,128]{2,0,1:T(8,128)}, u32[]{:S(2)}) copy-start(f32[16,12,128]{2,0,1:T(8,128)} %param.14) | copy-start | bytes 294916
  71.7 7.1 %copy-start.10 = (f32[16,12,128]{2,0,1:T(8,128)S(1)}, f32[16,12,128]{2,0,1:T(8,128)}, u32[]{:S(2)}) copy-start(f32[16,12,128]{2,0,1:T(8,128)} %param.13) | copy-start | bytes 294916
  71.7 7.1 %copy-start.16 = (f32[1,1,16,12,128]{4,2,3,1,0:T(8,128)S(1)}, f32[1,1,16,12,128]{4,2,3,1,0:T(8,128)}, u32[]{:S(2)}) copy-start(f32[1,1,16,12,128]{4,2,3,1,0:T(8,128)} %get-tuple-element.17) | copy-start | bytes 294916
  71.7 7.1 %copy-start.17 = (f32[1,1,16,12,128]{4,2,3,1,0:T(8,128)S(1)}, f32[1,1,16,12,128]{4,2,3,1,0:T(8,128)}, u32[]{:S(2)}) copy-start(f32[1,1,16,12,128]{4,2,3,1,0:T(8,128)} %get-tuple-element.18) | copy-start | bytes 294916
  71.7 19.6 %all-to-all-start.2 = ((f32[2,4,1,192,128]{4,1,0,2,3:T(4,128)}), f32[2,4,1,192,128]{4,1,0,2,3:T(4,128)}, u32[]{:S(2)}, u32[]{:S(2)}) async-start(f32[2,4,1,192,128]{4,1,0,2,3:T(4,128)} %copy.52), calls=%async_computation.2 | async-start | bytes 1572864 | tf_op jit(solution)/shard_map/all_to_all | solution.py:191
  78.8 2.3 %copy-start.11 = (f32[16,12,128]{2,0,1:T(8,128)S(1)}, f32[16,12,128]{2,0,1:T(8,128)}, u32[]{:S(2)}) copy-start(f32[16,12,128]{2,0,1:T(8,128)} %param.13) | copy-start | bytes 294916
  80.1 0.9 copy-start.3
  91.4 1.8 %copy-start.4 = (f32[2,5,16,12,128]{4,2,3,1,0:T(8,128)S(1)}, f32[2,5,16,12,128]{4,2,3,1,0:T(8,128)}, u32[]{:S(2)}) copy-start(f32[2,5,16,12,128]{4,2,3,1,0:T(8,128)} %copy-done.3) | copy-start | bytes 2949124
  91.4 1.8 %copy-start.14 = (f32[1,1,16,12,128]{4,2,3,1,0:T(8,128)S(1)}, f32[1,1,16,12,128]{4,2,3,1,0:T(8,128)}, u32[]{:S(2)}) copy-start(f32[1,1,16,12,128]{4,2,3,1,0:T(8,128)} %get-tuple-element.16) | copy-start | bytes 294916
  91.4 1.8 %copy-start.15 = (f32[1,1,16,12,128]{4,2,3,1,0:T(8,128)S(1)}, f32[1,1,16,12,128]{4,2,3,1,0:T(8,128)}, u32[]{:S(2)}) copy-start(f32[1,1,16,12,128]{4,2,3,1,0:T(8,128)} %get-tuple-element.23) | copy-start | bytes 294916
  94.4 0.9 copy-start.12
  94.4 0.9 copy-start.13
where the time goes:
time: 98.3 us; the launch traced here: 97.6 us
  waiting for transfers between devices  26.8 us (27%)
  starting transfers between devices  26.1 us (27%)
  matrix products  16.1 us (16%)
  other arithmetic  15.4 us (16%)
  local copies, waits for them, and re-layouts  12.7 us (13%)
    ppermute x1, waiting for transfers between devices, with_halo(): before = lax.ppermute(last, axis, up)  11.4 us
    dot_general x1, matrix products, theta_derivatives(): slope_t = jnp.dot(work_fields, theta_first, precision=highest)  8.68 us
    all_to_all x1, waiting for transfers between devices, per_device(): lax.all_to_all(curve_r, 'pen', split_axis=3, concat_axis=2, tiled=True)  8.63 us
    ppermute x1, starting transfers between devices, with_halo(): after = lax.ppermute(initial, axis, down)  6.88 us
    ppermute x1, waiting for transfers between devices, with_halo(): after = lax.ppermute(initial, axis, down)  6.69 us
    all_to_all x1, starting transfers between devices, per_device(): lax.all_to_all(slope_r, 'pen', split_axis=3, concat_axis=2, tiled=True)  6.24 us
    all_to_all x1, starting transfers between devices, per_device(): lax.all_to_all(curve_r, 'pen', split_axis=3, concat_axis=2, tiled=True)  5.85 us
    dot_general x1, matrix products, theta_derivatives(): jnp.dot(work_fields[:, :4], azimuthal_second_derivative, precision=highest)  5.32 us
  transfers between devices with their start and end apart: 5, of which 3 were waited for; matrix products, arithmetic and copies ran while one was open for 28% of the time, Pallas kernels for 0%

commit v1 on v0

--- a/solution.py
+++ b/solution.py
@@ -164,6 +164,15 @@
     return jnp.stack([term_u, term_v, term_w, term_rho, term_p], axis=1)
 
 
+def pencil_terms(pencil, radial_first, radial_second, inv_radius):
+    raw = pencil[:10].reshape((2, 5) + pencil.shape[1:])
+    radial_mean, density, pressure = (pencil[10], pencil[11], pencil[12])
+    pencil_work = build_work(raw, density, pressure)
+    slope_r, curve_r = radial_derivatives(pencil_work, radial_first, radial_second)
+    terms = radial_terms(slope_r, curve_r, radial_mean, density, pressure, inv_radius)
+    return terms.reshape((10,) + terms.shape[2:])
+
+
 def per_device(fields, axial_mean, radial_mean, swirl_mean, density, pressure):
     planes = fields.shape[2]
     shard_rows = fields.shape[3]
@@ -177,20 +186,23 @@
     theta_np, theta_second_np = fourier_tables(grid_points)
     theta_first = jnp.asarray(theta_np.T, jnp.float32)
     azimuthal_second_derivative = jnp.asarray(theta_second_np.T, jnp.float32)
+    outgoing = jnp.concatenate(
+        [
+            fields.reshape((10,) + fields.shape[2:]),
+            radial_mean[None],
+            density[None],
+            pressure[None],
+        ],
+        axis=0,
+    )
+    pencil = lax.all_to_all(outgoing, "pen", split_axis=1, concat_axis=2, tiled=True)
+    radial_pencil = pencil_terms(pencil, radial_first, radial_second, inv_all)
+    radial_back = lax.all_to_all(radial_pencil, "pen", split_axis=2, concat_axis=1, tiled=True)
+    radial_component = radial_back.reshape(fields.shape)
     work_fields = build_work(fields, density, pressure)
     padded = with_halo(work_fields, (("ax", 2),), 4)
     slope_x, curve_x = axial_derivatives(padded, planes)
     slope_t, curve_t = theta_derivatives(work_fields, theta_first, azimuthal_second_derivative)
-    slope_r, curve_r = radial_derivatives(
-        lax.all_to_all(work_fields, "pen", split_axis=2, concat_axis=3, tiled=True),
-        radial_first,
-        radial_second,
-    )
-    slope_r, curve_r = (
-        lax.all_to_all(slope_r, "pen", split_axis=3, concat_axis=2, tiled=True),
-        lax.all_to_all(curve_r, "pen", split_axis=3, concat_axis=2, tiled=True),
-    )
-    radial_component = radial_terms(slope_r, curve_r, radial_mean, density, pressure, inv_local)
     return radial_component + other_terms(
         work_fields,
         slope_x,

time: 98.3 us -> 80.8 us (0.82)
  the two profiles are of different devices: /device:TPU:4 before, /device:TPU:1 now
where the time goes in v1:
time: 80.8 us; the launch traced here: 80.1 us
  starting transfers between devices  23.3 us (29%)
  waiting for transfers between devices  19.5 us (24%)
  other arithmetic  17.1 us (21%)
  local copies, waits for them, and re-layouts  13.4 us (17%)
  matrix products  6.39 us (8%)
    all_to_all x1, starting transfers between devices, per_device(): lax.all_to_all(outgoing, 'pen', split_axis=1, concat_axis=2, tiled=True)  10.4 us
    all_to_all x1, waiting for transfers between devices, per_device(): lax.all_to_all(radial_pencil, 'pen', split_axis=2, concat_axis=1, tiled=T...  9.76 us
    all_to_all x1, waiting for transfers between devices, per_device(): lax.all_to_all(outgoing, 'pen', split_axis=1, concat_axis=2, tiled=True)  9.75 us
    ppermute x1, starting transfers between devices, with_halo(): before = lax.ppermute(last, axis, up)  6.84 us
    all_to_all x1, starting transfers between devices, per_device(): lax.all_to_all(radial_pencil, 'pen', split_axis=2, concat_axis=1, tiled=T...  4.78 us
    unnamed x8, other arithmetic  4.7 us
    all_to_all x1, other arithmetic, per_device(): lax.all_to_all(radial_pencil, 'pen', split_axis=2, concat_axis=1, tiled=T...  3.78 us
    dot_general x1, matrix products, theta_derivatives(): slope_t = jnp.dot(work_fields, theta_first, precision=highest)  2.97 us
  transfers between devices with their start and end apart: 4, of which 2 were waited for; matrix products, arithmetic and copies ran while one was open for 21% of the time, Pallas kernels for 0%

profile of v1, /device:TPU:1, one launch (start us, length us, event | category | flops | bytes accessed | tf_op | source)
XLA Modules:
  0.0 80.1 jit_solution(15807028151501583979)
XLA Ops:
  0.0 1.1 %slice.297 = f32[2,2,16,12,128]{4,2,3,1,0:T(8,128)S(1)} slice(f32[2,5,16,12,128]{4,2,3,1,0:T(8,128)} %param.11), slice={[0:2], [3:5], [0:16], [0:12], [0:128]} | slice | bytes 786432 | tf_op jit(solution)/shard_map/slice | solution.py:72
  1.2 1.2 %slice.294 = f32[2,3,16,12,128]{4,2,3,1,0:T(8,128)S(1)} slice(f32[2,5,16,12,128]{4,2,3,1,0:T(8,128)} %param.11), slice={[0:2], [0:3], [0:16], [0:12], [0:128]} | slice | bytes 1179648 | tf_op jit(solution)/shard_map/slice | solution.py:72
  2.5 0.9 %pad_maximum_fusion.5 = (f32[2,6,4,12,128]{4,2,3,1,0:T(4,128)}, f32[2,6,4,12,128]{4,2,3,1,0:T(4,128)}) fusion(f32[2,2,16,12,128]{4,2,3,1,0:T(8,128)S(1)} %slice.297, f32[2,1,16,12,128]{4,2,3,1,0:T(8,128)S(1)} %divide_subtract_fusion, f32[2,3,16,12,128]{4,2,3,1,0:T(8,128)S(1)} %slice.294), kind=kLoop, calls=%fused_computation.53 | loop fusion | flops 294912 | bytes 1769472 | tf_op jit(solution)/shard_map/slice | solution.py:25
  3.5 1.3 %collective-permute-start = (f32[2,6,4,12,128]{4,2,3,1,0:T(4,128)}, f32[2,6,4,12,128]{4,2,3,1,0:T(4,128)}, u32[]{:S(2)}, u32[]{:S(2)}) collective-permute-start(f32[2,6,4,12,128]{4,2,3,1,0:T(4,128)} %get-tuple-element.14), channel_id=1, source_target_pairs={{16,0},{32,16},{48,32},{64,48},{80,64},{96,80},{112,96},{128,112},... | collective-permute-start | bytes 884744 | tf_op jit(solution)/shard_map/ppermute | solution.py:27
  4.8 6.8 %collective-permute-start.1 = (f32[2,6,4,12,128]{4,2,3,1,0:T(4,128)}, f32[2,6,4,12,128]{4,2,3,1,0:T(4,128)}, u32[]{:S(2)}, u32[]{:S(2)}) collective-permute-start(f32[2,6,4,12,128]{4,2,3,1,0:T(4,128)} %get-tuple-element.15), channel_id=1, source_target_pairs={{0,16},{16,32},{32,48},{48,64},{64,80},{80,96},{96,112},{112,128},... | collective-permute-start | bytes 884744 | tf_op jit(solution)/shard_map/ppermute | solution.py:26
  11.7 1.9 %copy.34 = f32[13,16,12,128]{3,0,2,1:T(8,128)} copy(f32[13,16,12,128]{3,1,2,0:T(8,128)S(1)} %pad_maximum_fusion.1) | data formatting | bytes 2555904 | tf_op jit(solution)/shard_map/concatenate | solution.py:189
  13.7 10.4 %all-to-all-start = ((f32[13,16,12,128]{3,0,2,1:T(8,128)}), f32[13,16,12,128]{3,0,2,1:T(8,128)S(1)}, u32[]{:S(2)}, u32[]{:S(2)}) async-start(f32[13,16,12,128]{3,0,2,1:T(8,128)} %copy.34), calls=%async_computation | async-start | bytes 3145728 | tf_op jit(solution)/shard_map/all_to_all | solution.py:198
  24.2 1.7 %broadcast_multiply_fusion.3 = (f32[16,12,128]{2,0,1:T(8,128)}, f32[16,12,128]{2,0,1:T(8,128)S(1)}, f32[16,12,128]{2,0,1:T(8,128)S(1)}) fusion(f32[16,12,128]{2,0,1:T(8,128)} %param.14, f32[12]{0:T(128)S(1)} %get-tuple-element.28, f32[12]{0:T(128)S(1)} %get-tuple-element.30, f32[16,12,128]{2,0,1:T(8,128)} %param.12), kind=kLoop, calls=%fused_computation.120 | loop fusion | flops 73728 | bytes 491616 | tf_op jit(solution)/shard_map/mul | solution.py:147
  25.8 0.6 broadcast_multiply_fusion.2
  26.5 0.9 %slice_multiply_fusion.11 = (f32[1,1,16,12,128]{4,2,3,1,0:T(8,128)}, f32[1,1,16,12,128]{4,2,3,1,0:T(8,128)}, f32[1,1,16,12,128]{4,2,3,1,0:T(8,128)}, f32[1,1,16,...) fusion(f32[2,5,16,12,128]{4,2,3,1,0:T(8,128)S(1)} %copy-done), kind=kLoop, calls=%fused_computation.110 | loop fusion | flops 245760 | bytes 1966080 | tf_op jit(solution)/shard_map/mul | solution.py:107
  27.4 1.5 %pad_maximum_fusion = (f32[2,6,20,12,128]{4,2,3,1,0:T(8,128)S(1)}, f32[2,6,20,12,128]{4,2,3,1,0:T(8,128)S(1)}) fusion(f32[2,6,4,12,128]{4,2,3,1,0:T(4,128)} %collective-permute-done, f32[2,2,16,12,128]{4,2,3,1,0:T(8,128)S(1)} %copy-done.4, f32[2,1,16,12,128]{4,2,3,1,0:T(8,128)S(1)} %divide_subtract_fusion, f32[2,3,16,12,128]{4,2,3,1,0:T(8,128)S(1)} %slice.294, ...), kind=kLoop, calls=%fused_computation | loop fusion | flops 2211840 | bytes 4718592 | tf_op jit(solution)/shard_map/concatenate | solution.py:28
  28.9 3.0 %multiply_add_fusion = (f32[2,6,16,12,128]{4,2,3,1,0:T(8,128)S(1)}, f32[2,6,16,12,128]{4,2,3,1,0:T(8,128)S(1)}, f32[2,6,16,12,128]{4,2,3,1,0:T(8,128)}) fusion(f32[16,12,128]{2,0,1:T(8,128)S(1)} %get-tuple-element.27, f32[16,12,128]{2,0,1:T(8,128)S(1)} %get-tuple-element.34, f32[2,6,20,12,128]{4,2,3,1,0:T(8,128)S(1)} %get-tuple-element.13, ...), kind=kOutput, calls=%fused_computation.30 | convolution fusion | flops 457703424 | bytes 14417920 | tf_op jit(solution)/shard_map/dot_general | solution.py:95
  32.0 0.8 copy-done.26
  32.8 1.4 %fusion = f32[2,4,16,12,128]{4,2,3,1,0:T(8,128)S(1)} fusion(f32[128,128,1,1,1]{1,0,4,3,2:T(8,128)S(1)} %copy-done.26, f32[2,6,20,12,128]{4,2,3,1,0:T(8,128)S(1)} %get-tuple-element.13, f32[2,6,20,12,128]{4,2,3,1,0:T(8,128)S(1)} %get-tuple-element.12, f32[2,1,16,12,128]{4,2,3,1,0:T(8,128)S(1)} %divide_subtract_fusion, f32[2,3,16,12,128]{4,2,3,1,0:T(8,128)S(1)} %slice.294, ...), kind=kOutput, calls=%fused_computation.5 | convolution fusion | flops 305528832 | bytes 8716800 | tf_op jit(solution)/shard_map/dot_general | solution.py:96
  34.2 0.9 %copy-done.10 = f32[2,4,16,12,128]{4,2,3,1,0:T(8,128)} copy-done((f32[2,4,16,12,128]{4,2,3,1,0:T(8,128)}, f32[2,4,16,12,128]{4,2,3,1,0:T(8,128)S(1)}, u32[]{:S(2)}) %copy-start.10) | copy-done | bytes 786456
  35.0 0.7 fusion.49
  35.8 9.7 %all-to-all-done = f32[13,16,12,128]{3,0,2,1:T(8,128)S(1)} async-done(((f32[13,16,12,128]{3,0,2,1:T(8,128)}), f32[13,16,12,128]{3,0,2,1:T(8,128)S(1)}, u32[]{:S(2)}, u32[]{:S(2)}) %all-to-all-start) | async-done | bytes 1277984 | tf_op jit(solution)/shard_map/all_to_all | solution.py:198
  45.5 1.4 %copy.35 = f32[10,16,12,128]{3,2,1,0:T(8,128)} copy(f32[10,16,12,128]{3,0,2,1:T(8,128)S(1)} %bitcast.46) | data formatting | bytes 1966080 | tf_op jit(solution)/shard_map/slice | solution.py:168
  46.9 1.4 %reshape.205 = f32[2,5,1,192,128]{4,3,1,0,2:T(8,128)S(1)} reshape(f32[10,16,12,128]{3,2,1,0:T(8,128)} %copy.35) | data formatting | bytes 1966080 | tf_op jit(solution)/shard_map/reshape | solution.py:168
  48.8 0.6 copy-done.24
  49.4 1.2 %broadcast_multiply_fusion.1 = (f32[2,6,1,192,128]{4,3,1,0,2:T(8,128)S(1)}, f32[2,6,1,192,128]{4,3,1,0,2:T(8,128)S(1)}) fusion(f32[192,128]{1,0:T(8,128)S(1)} %bitcast.58, f32[192,192,1,1]{1,0,3,2:T(8,128)S(1)} %copy-done.24, f32[2,2,1,192,128]{4,3,1,0,2:T(8,128)S(1)} %slice.347, f32[2,1,1,192,128]{4,3,1,0,2:T(8,128)S(1)} %fusion.62, ...), kind=kOutput, calls=%fused_computation.51 | convolution fusion | flops 680361984 | bytes 3784704 | tf_op jit(solution)/shard_map/sj,abxjt->abxst/dot_general | solution.py:101
  50.6 0.9 %fusion.1 = f32[2,4,1,192,128]{4,3,1,0,2:T(8,128)S(1)} fusion(f32[192,192,1,1]{1,0,3,2:T(8,128)S(1)} %copy-done.23, f32[2,6,1,192,128]{4,3,1,0,2:T(8,128)S(1)} %get-tuple-element.33, f32[2,1,1,192,128]{4,3,1,0,2:T(8,128)S(1)} %fusion.62, f32[2,3,1,192,128]{4,3,1,0,2:T(8,128)S(1)} %slice.342, f32[192]{0:T(256)S(1)} %copy-done.25), kind=kOutput, calls=%fused_computation.7 | convolution fusion | flops 453574656 | bytes 2507520 | tf_op jit(solution)/shard_map/sj,abxjt->abxst/dot_general | solution.py:102
  51.6 2.0 %copy.36 = f32[10,1,192,128]{3,1,0,2:T(1,128)} copy(f32[10,1,192,128]{3,2,0,1:T(8,128)S(1)} %bitcast.53) | data formatting | bytes 1966080 | tf_op jit(solution)/shard_map/reshape | solution.py:173
  53.6 4.8 %all-to-all-start.1 = ((f32[10,1,192,128]{3,1,0,2:T(1,128)}), f32[10,1,192,128]{3,1,0,2:T(1,128)S(1)}, u32[]{:S(2)}, u32[]{:S(2)}) async-start(f32[10,1,192,128]{3,1,0,2:T(1,128)} %copy.36), calls=%async_computation.1 | async-start | bytes 1966080 | tf_op jit(solution)/shard_map/all_to_all | solution.py:200
  58.5 1.4 %fusion.46 = f32[2,5,16,12,128]{4,2,3,1,0:T(8,128)S(1)} fusion(f32[2,5,16,12,128]{4,2,3,1,0:T(8,128)S(1)} %copy-done.6, f32[2,4,16,12,128]{4,2,3,1,0:T(8,128)} %copy-done.10, f32[2,6,16,12,128]{4,2,3,1,0:T(8,128)} %copy-done.8, f32[1,1,16,12,128]{4,2,3,1,0:T(8,128)S(1)} %copy-done.22, f32[1,1,16,12,128]{4,2,3,1,0:T(8,128)} %get-tuple-element.21, ...), kind=kLoop, calls=%fused_computation.78 | loop fusion | flops 491520 | bytes 1475072
  60.1 1.2 %fusion.40 = f32[2,5,16,12,128]{4,2,3,1,0:T(8,128)S(1)} fusion(f32[2,5,16,12,128]{4,2,3,1,0:T(8,128)S(1)} %fusion.46, f32[2,6,16,12,128]{4,2,3,1,0:T(8,128)} %get-tuple-element.31, f32[2,4,16,12,128]{4,2,3,1,0:T(8,128)} %copy-done.10, f32[2,6,16,12,128]{4,2,3,1,0:T(8,128)S(1)} %copy-done.9, f32[1,1,16,12,128]{4,2,3,1,0:T(8,128)S(1)} %copy-done.14, ...), kind=kLoop, calls=%fused_computation.69 | loop fusion | flops 786432 | bytes 1868800
  61.4 1.2 %fusion.34 = (f32[2,5,16,12,128]{4,2,3,1,0:T(8,128)S(1)}, f32[2,1,16,12,128]{4,2,3,1,0:T(8,128)S(1)}) fusion(f32[2,5,16,12,128]{4,2,3,1,0:T(8,128)S(1)} %fusion.40, f32[2,6,16,12,128]{4,2,3,1,0:T(8,128)S(1)} %copy-done.9, f32[1,1,16,12,128]{4,2,3,1,0:T(8,128)S(1)} %copy-done.21, f32[1,1,16,12,128]{4,2,3,1,0:T(8,128)S(1)} %copy-done.20, ...), kind=kLoop, calls=%fused_computation.62 | loop fusion | flops 344064 | bytes 1475072
  62.6 1.0 %fusion.31 = f32[2,5,16,12,128]{4,2,3,1,0:T(8,128)S(1)} fusion(f32[2,5,16,12,128]{4,2,3,1,0:T(8,128)S(1)} %get-tuple-element.5, f32[2,4,16,12,128]{4,2,3,1,0:T(8,128)} %copy-done.10, f32[2,6,16,12,128]{4,2,3,1,0:T(8,128)S(1)} %copy-done.9, f32[1,1,16,12,128]{4,2,3,1,0:T(8,128)S(1)} %copy-done.18, f32[1,1,16,12,128]{4,2,3,1,0:T(8,128)S(1)} %copy-done.17, ...), kind=kLoop, calls=%fused_computation.56 | loop fusion | flops 294912 | bytes 1081344 | tf_op jit(solution)/shard_map/stack | solution.py:164
  63.6 9.8 %all-to-all-done.1 = f32[10,1,192,128]{3,1,0,2:T(1,128)S(1)} async-done(((f32[10,1,192,128]{3,1,0,2:T(1,128)}), f32[10,1,192,128]{3,1,0,2:T(1,128)S(1)}, u32[]{:S(2)}, u32[]{:S(2)}) %all-to-all-start.1) | async-done | bytes 983072 | tf_op jit(solution)/shard_map/all_to_all | solution.py:200
  73.4 3.8 %reduce = f32[10,192,128]{2,0,1:T(8,128)} reduce(f32[10,1,192,128]{3,1,0,2:T(1,128)S(1)} %all-to-all-done.1, f32[]{:T(128)} %constant.74), dimensions={1}, to_apply=%all_to_all.5.reduce_sub_computation | reduce | bytes 1966084 | tf_op jit(solution)/shard_map/all_to_all | solution.py:200
  77.2 1.4 %reshape.214 = f32[2,5,16,12,128]{4,1,0,3,2:T(8,128)S(1)} reshape(f32[10,192,128]{2,0,1:T(8,128)} %reduce) | data formatting | bytes 1966080 | tf_op jit(solution)/shard_map/reshape | solution.py:201
  78.6 1.5 %copy_add_fusion = f32[2,5,16,12,128]{4,2,3,1,0:T(8,128)} fusion(f32[2,5,16,12,128]{4,2,3,1,0:T(8,128)S(1)} %fusion.31, f32[2,5,16,12,128]{4,1,0,3,2:T(8,128)S(1)} %reshape.214), kind=kLoop, calls=%fused_computation.31 | loop fusion | flops 245760 | bytes 2949120 | tf_op jit(solution)/shard_map/add | solution.py:206
  (71 shorter events, 1.1 us)
Async XLA Ops:
  0.0 2.4 %copy-start = (f32[2,5,16,12,128]{4,2,3,1,0:T(8,128)S(1)}, f32[2,5,16,12,128]{4,2,3,1,0:T(8,128)}, u32[]{:S(2)}) copy-start(f32[2,5,16,12,128]{4,2,3,1,0:T(8,128)} %param.11) | copy-start | bytes 2949124
  0.0 2.4 %copy-start.1 = (f32[16,12,128]{2,0,1:T(8,128)S(1)}, f32[16,12,128]{2,0,1:T(8,128)}, u32[]{:S(2)}) copy-start(f32[16,12,128]{2,0,1:T(8,128)} %param.15) | copy-start | bytes 294916
  0.0 2.5 %copy-start.7 = (f32[16,12,128]{2,0,1:T(8,128)S(1)}, f32[16,12,128]{2,0,1:T(8,128)}, u32[]{:S(2)}) copy-start(f32[16,12,128]{2,0,1:T(8,128)} %param.16) | copy-start | bytes 294916
  1.1 1.4 %copy-start.3 = (f32[2,2,16,12,128]{4,2,3,1,0:T(8,128)}, f32[2,2,16,12,128]{4,2,3,1,0:T(8,128)S(1)}, u32[]{:S(2)}) copy-start(f32[2,2,16,12,128]{4,2,3,1,0:T(8,128)S(1)} %slice.297) | copy-start | bytes 1179652
  2.5 9.1 %copy-start.11 = (f32[16,12,128]{2,0,1:T(8,128)S(1)}, f32[16,12,128]{2,0,1:T(8,128)}, u32[]{:S(2)}) copy-start(f32[16,12,128]{2,0,1:T(8,128)} %param.13) | copy-start | bytes 294916
  3.5 23.9 %collective-permute-start = (f32[2,6,4,12,128]{4,2,3,1,0:T(4,128)}, f32[2,6,4,12,128]{4,2,3,1,0:T(4,128)}, u32[]{:S(2)}, u32[]{:S(2)}) collective-permute-start(f32[2,6,4,12,128]{4,2,3,1,0:T(4,128)} %get-tuple-element.14), channel_id=1, source_target_pairs={{16,0},{32,16},{48,32},{64,48},{80,64},{96,80},{112,96},{128,112},... | collective-permute-start | bytes 884744 | tf_op jit(solution)/shard_map/ppermute | solution.py:27
  4.8 22.6 %collective-permute-start.1 = (f32[2,6,4,12,128]{4,2,3,1,0:T(4,128)}, f32[2,6,4,12,128]{4,2,3,1,0:T(4,128)}, u32[]{:S(2)}, u32[]{:S(2)}) collective-permute-start(f32[2,6,4,12,128]{4,2,3,1,0:T(4,128)} %get-tuple-element.15), channel_id=1, source_target_pairs={{0,16},{16,32},{32,48},{48,64},{64,80},{80,96},{96,112},{112,128},... | collective-permute-start | bytes 884744 | tf_op jit(solution)/shard_map/ppermute | solution.py:26
  13.7 10.4 %copy-start.25 = (f32[192]{0:T(256)S(1)}, f32[192]{0:T(256)}, u32[]{:S(2)}) copy-start(f32[192]{0:T(256)} %constant.24.clone) | copy-start | bytes 2308
  13.7 31.8 %all-to-all-start = ((f32[13,16,12,128]{3,0,2,1:T(8,128)}), f32[13,16,12,128]{3,0,2,1:T(8,128)S(1)}, u32[]{:S(2)}, u32[]{:S(2)}) async-start(f32[13,16,12,128]{3,0,2,1:T(8,128)} %copy.34), calls=%async_computation | async-start | bytes 3145728 | tf_op jit(solution)/shard_map/all_to_all | solution.py:198
  25.8 1.6 %copy-start.4 = (f32[2,2,16,12,128]{4,2,3,1,0:T(8,128)S(1)}, f32[2,2,16,12,128]{4,2,3,1,0:T(8,128)}, u32[]{:S(2)}) copy-start(f32[2,2,16,12,128]{4,2,3,1,0:T(8,128)} %copy-done.3) | copy-start | bytes 1179652
  27.4 1.5 %copy-start.27 = (f32[128,128,1,1,1]{1,0,4,3,2:T(8,128)S(1)}, f32[128,128,1,1,1]{1,0,4,3,2:T(8,128)}, u32[]{:S(2)}) copy-start(f32[128,128,1,1,1]{1,0,4,3,2:T(8,128)} %constant.72) | copy-start | bytes 196612
  31.9 2.3 %copy-start.8 = (f32[2,6,16,12,128]{4,2,3,1,0:T(8,128)}, f32[2,6,16,12,128]{4,2,3,1,0:T(8,128)S(1)}, u32[]{:S(2)}) copy-start(f32[2,6,16,12,128]{4,2,3,1,0:T(8,128)S(1)} %get-tuple-element.7) | copy-start | bytes 3538948
  31.9 0.9 %copy-start.26 = (f32[128,128,1,1,1]{1,0,4,3,2:T(8,128)S(1)}, f32[128,128,1,1,1]{1,0,4,3,2:T(8,128)}, u32[]{:S(2)}) copy-start(f32[128,128,1,1,1]{1,0,4,3,2:T(8,128)} %constant.73) | copy-start | bytes 196612
  32.0 2.2 %copy-start.5 = (f32[2,6,16,12,128]{4,2,3,1,0:T(8,128)}, f32[2,6,16,12,128]{4,2,3,1,0:T(8,128)S(1)}, u32[]{:S(2)}) copy-start(f32[2,6,16,12,128]{4,2,3,1,0:T(8,128)S(1)} %broadcast_multiply_fusion) | copy-start | bytes 3538948
  34.1 0.9 %copy-start.10 = (f32[2,4,16,12,128]{4,2,3,1,0:T(8,128)}, f32[2,4,16,12,128]{4,2,3,1,0:T(8,128)S(1)}, u32[]{:S(2)}) copy-start(f32[2,4,16,12,128]{4,2,3,1,0:T(8,128)S(1)} %fusion) | copy-start | bytes 2359300
  48.4 0.9 %copy-start.24 = (f32[192,192,1,1]{1,0,3,2:T(8,128)S(1)}, f32[192,192,1,1]{1,0,3,2:T(8,128)}, u32[]{:S(2)}) copy-start(f32[192,192,1,1]{1,0,3,2:T(8,128)} %constant.70) | copy-start | bytes 442372
  49.4 1.2 %copy-start.23 = (f32[192,192,1,1]{1,0,3,2:T(8,128)S(1)}, f32[192,192,1,1]{1,0,3,2:T(8,128)}, u32[]{:S(2)}) copy-start(f32[192,192,1,1]{1,0,3,2:T(8,128)} %constant.71) | copy-start | bytes 442372
  53.6 4.8 %copy-start.6 = (f32[2,5,16,12,128]{4,2,3,1,0:T(8,128)S(1)}, f32[2,5,16,12,128]{4,2,3,1,0:T(8,128)}, u32[]{:S(2)}) copy-start(f32[2,5,16,12,128]{4,2,3,1,0:T(8,128)} %fusion.49) | copy-start | bytes 2949124
  53.6 4.9 %copy-start.19 = (f32[16,12,128]{2,0,1:T(8,128)S(1)}, f32[16,12,128]{2,0,1:T(8,128)}, u32[]{:S(2)}) copy-start(f32[16,12,128]{2,0,1:T(8,128)} %get-tuple-element.26) | copy-start | bytes 294916
  53.6 4.9 %copy-start.22 = (f32[1,1,16,12,128]{4,2,3,1,0:T(8,128)S(1)}, f32[1,1,16,12,128]{4,2,3,1,0:T(8,128)}, u32[]{:S(2)}) copy-start(f32[1,1,16,12,128]{4,2,3,1,0:T(8,128)} %get-tuple-element.20) | copy-start | bytes 294916
  53.6 6.3 %copy-start.14 = (f32[1,1,16,12,128]{4,2,3,1,0:T(8,128)S(1)}, f32[1,1,16,12,128]{4,2,3,1,0:T(8,128)}, u32[]{:S(2)}) copy-start(f32[1,1,16,12,128]{4,2,3,1,0:T(8,128)} %get-tuple-element.18) | copy-start | bytes 294916
  53.6 6.3 %copy-start.15 = (f32[1,1,16,12,128]{4,2,3,1,0:T(8,128)S(1)}, f32[1,1,16,12,128]{4,2,3,1,0:T(8,128)}, u32[]{:S(2)}) copy-start(f32[1,1,16,12,128]{4,2,3,1,0:T(8,128)} %get-tuple-element.19) | copy-start | bytes 294916
  53.6 19.7 %all-to-all-start.1 = ((f32[10,1,192,128]{3,1,0,2:T(1,128)}), f32[10,1,192,128]{3,1,0,2:T(1,128)S(1)}, u32[]{:S(2)}, u32[]{:S(2)}) async-start(f32[10,1,192,128]{3,1,0,2:T(1,128)} %copy.36), calls=%async_computation.1 | async-start | bytes 1966080 | tf_op jit(solution)/shard_map/all_to_all | solution.py:200
  58.4 1.5 %copy-start.2 = (f32[16,12,128]{2,0,1:T(8,128)S(1)}, f32[16,12,128]{2,0,1:T(8,128)}, u32[]{:S(2)}) copy-start(f32[16,12,128]{2,0,1:T(8,128)} %param.15) | copy-start | bytes 294916
  58.4 1.7 %copy-start.9 = (f32[2,6,16,12,128]{4,2,3,1,0:T(8,128)S(1)}, f32[2,6,16,12,128]{4,2,3,1,0:T(8,128)}, u32[]{:S(2)}) copy-start(f32[2,6,16,12,128]{4,2,3,1,0:T(8,128)} %copy-done.8) | copy-start | bytes 3538948
  58.4 1.6 %copy-start.12 = (f32[16,12,128]{2,0,1:T(8,128)S(1)}, f32[16,12,128]{2,0,1:T(8,128)}, u32[]{:S(2)}) copy-start(f32[16,12,128]{2,0,1:T(8,128)} %param.13) | copy-start | bytes 294916
  58.4 1.6 %copy-start.13 = (f32[16,12,128]{2,0,1:T(8,128)S(1)}, f32[16,12,128]{2,0,1:T(8,128)}, u32[]{:S(2)}) copy-start(f32[16,12,128]{2,0,1:T(8,128)} %param.14) | copy-start | bytes 294916
  59.9 1.5 %copy-start.20 = (f32[1,1,16,12,128]{4,2,3,1,0:T(8,128)S(1)}, f32[1,1,16,12,128]{4,2,3,1,0:T(8,128)}, u32[]{:S(2)}) copy-start(f32[1,1,16,12,128]{4,2,3,1,0:T(8,128)} %get-tuple-element.17) | copy-start | bytes 294916
  59.9 1.5 %copy-start.21 = (f32[1,1,16,12,128]{4,2,3,1,0:T(8,128)S(1)}, f32[1,1,16,12,128]{4,2,3,1,0:T(8,128)}, u32[]{:S(2)}) copy-start(f32[1,1,16,12,128]{4,2,3,1,0:T(8,128)} %get-tuple-element.22) | copy-start | bytes 294916
  61.3 1.3 %copy-start.16 = (f32[16,12,128]{2,0,1:T(8,128)S(1)}, f32[16,12,128]{2,0,1:T(8,128)}, u32[]{:S(2)}) copy-start(f32[16,12,128]{2,0,1:T(8,128)} %broadcast_multiply_fusion.2) | copy-start | bytes 294916
  61.3 1.3 %copy-start.17 = (f32[1,1,16,12,128]{4,2,3,1,0:T(8,128)S(1)}, f32[1,1,16,12,128]{4,2,3,1,0:T(8,128)}, u32[]{:S(2)}) copy-start(f32[1,1,16,12,128]{4,2,3,1,0:T(8,128)} %get-tuple-element.16) | copy-start | bytes 294916
  61.4 1.3 %copy-start.18 = (f32[1,1,16,12,128]{4,2,3,1,0:T(8,128)S(1)}, f32[1,1,16,12,128]{4,2,3,1,0:T(8,128)}, u32[]{:S(2)}) copy-start(f32[1,1,16,12,128]{4,2,3,1,0:T(8,128)} %get-tuple-element.25) | copy-start | bytes 294916
